TPU v7x, 256 devices: a whole 4x4x8 slice. The times are simulated.
256 devices in a mesh: tm: 16 (over y, x), space: 16 (over z, core).
Axes of the slice: x: 4, y: 4, z: 8, core: 2. Of those that a mesh axis runs over, the one named last changes fastest.
Arguments:
- query_heads: bfloat16 [32, 64, 64, 2240], P('tm', 'space'), may hold values from -10.5 to 10.5
- key_heads: bfloat16 [32, 64, 64, 2240], P('tm', 'space'), may hold values from -10.5 to 10.5
- value_heads: bfloat16 [32, 64, 64, 2240], P('tm', 'space'), may hold values from -12 to 12
- head_gain: float32 [2240], replicated, may hold values from 0.1 to 1.9
- spatial_kernel: float32 [9, 2240], replicated, may hold values from -2 to 2
- temporal_kernel: float32 [3, 2240], replicated, may hold values from -3.5 to 3.5
- out_weight: bfloat16 [2240, 2240], P('space', 'tm'), may hold values from -0.125 to 0.125
Outputs:
- mixed_out: bfloat16 [32, 64, 64, 2240], P('tm', 'space')
All inputs are finite; a program needn't handle non-finite values.
Results may differ from a plain program's by a relative error of at most 0.0057.
Values may be sent and summed in bfloat16 or wider, within the bound.
No kernel may reach another device: no remote copies, remote signals or barrier semaphores. Data moves between devices by JAX's collectives and lax.ppermute only.
A program may use at most 128 MiB of HBM per device.

v0:
```python
import jax
import jax.numpy as jnp
from jax import lax
from jax.sharding import PartitionSpec as P

HEADS = 20
HEAD_DIM = 112
epsilon = 1e-06


def entering(part, axis, combine, identity):
    place = lax.axis_index(axis)
    gathered = lax.all_gather(part, axis)
    state = jnp.zeros_like(part) + jnp.asarray(identity, part.dtype)

    def one(hop, state):
        return combine(state, lax.dynamic_index_in_dim(gathered, hop, 0, False))

    return lax.fori_loop(0, place, one, state)


def extended(block, sides, width):
    for axis, dim in sides:
        count = lax.axis_size(axis)
        forward = [(i, i + 1) for i in range(count - 1)]
        backward = [(target, source) for source, target in forward]
        low = lax.ppermute(
            lax.slice_in_dim(block, block.shape[dim] - width, None, axis=dim), axis, forward
        )
        high = lax.ppermute(lax.slice_in_dim(block, 0, width, axis=dim), axis, backward)
        block = jnp.concatenate([low, block, high], axis=dim)
    return block


def from_behind(block, axis, distance):
    devices = range(lax.axis_size(axis))
    route = [(i - distance, i) for i in devices if i - distance in devices]
    return lax.ppermute(block, axis, route)


def add_states(earlier, latter):
    return earlier + latter


def spatial_conv(padded, spatial_kernel):
    frame_count = padded.shape[0]
    row_count = padded.shape[1] - 2
    col_count = padded.shape[2]
    widened = jnp.pad(padded, ((0, 0), (0, 0), (1, 1), (0, 0)))
    summed = jnp.zeros((frame_count, row_count, col_count, padded.shape[3]), jnp.float32)
    for row_step in range(3):
        for col_step in range(3):
            summed = summed + spatial_kernel[3 * row_step + col_step] * widened[
                :, row_step : row_step + row_count, col_step : col_step + col_count
            ].astype(jnp.float32)
    return summed.astype(jnp.bfloat16)


def per_device(
    query_heads, key_heads, value_heads, head_gain, spatial_kernel, temporal_kernel, out_weight
):
    frame_count, row_count, col_count, model_width = query_heads.shape
    token_count = frame_count * row_count * col_count
    queries = query_heads.reshape(token_count, HEADS, HEAD_DIM)
    key_rows = key_heads.reshape(token_count, HEADS, HEAD_DIM)
    value_rows = value_heads.reshape(token_count, HEADS, HEAD_DIM)
    local_state = jnp.einsum(
        "thd,the->hde", jnp.maximum(key_rows, 0), value_rows, preferred_element_type=jnp.float32
    )
    summed = lax.psum(local_state, "space")
    earlier = entering(summed, "tm", add_states, jnp.zeros_like(summed))
    state_low = (earlier + summed).astype(jnp.bfloat16)
    attended = jnp.einsum(
        "thd,hde->the", jnp.maximum(queries, 0), state_low, preferred_element_type=jnp.float32
    )
    mean_square = jnp.mean(attended * attended, axis=-1, keepdims=True)
    normed = (attended * lax.rsqrt(mean_square + epsilon)).reshape(
        frame_count, row_count, col_count, model_width
    ) * head_gain
    padded = extended(value_heads, (("space", 1),), 1)
    spatial = spatial_conv(padded, spatial_kernel)
    earlier_frames = from_behind(spatial, "tm", 1)
    window = jnp.concatenate([earlier_frames, spatial], axis=0)
    temporal = jnp.zeros(normed.shape, jnp.float32)
    for back_step in range(3):
        temporal = temporal + temporal_kernel[back_step] * window[
            2 - back_step : 2 - back_step + frame_count
        ].astype(jnp.float32)
    mixed = (normed + temporal).astype(jnp.bfloat16).reshape(token_count, model_width)
    weight_band = lax.all_gather(out_weight, "tm", axis=1, tiled=True)
    projected = jnp.dot(
        mixed,
        lax.all_gather(weight_band, "space", axis=0, tiled=True),
        preferred_element_type=jnp.float32,
    )
    return projected.astype(jnp.bfloat16).reshape(frame_count, row_count, col_count, model_width)


def solution(mesh):
    placed = (
        P("tm", "space", None, None),
        P("tm", "space", None, None),
        P("tm", "space", None, None),
        P(),
        P(),
        P(),
        P("space", "tm"),
    )
    return jax.shard_map(
        per_device,
        mesh=mesh,
        in_specs=placed,
        out_specs=P("tm", "space", None, None),
        check_vma=False,
    )
```

profile of v0, /device:TPU:30, one launch (start us, length us, event | category | flops | bytes accessed | tf_op | source)
XLA Modules:
  0.0 405.4 jit_solution(10233113582889997337)
XLA Ops:
  6.5 3.4 broadcast_maximum_fusion.1
  9.9 6.5 %max.13 = bf16[512,20,112]{2,1,0:T(8,128)(2,1)} reshape(bf16[2,4,64,2240]{3,2,1,0:T(8,128)(2,1)} %broadcast_maximum_fusion.1) | data formatting | bytes 4587520 | tf_op jit(solution)/shard_map/max | solution.py:68
  16.5 4.3 %reshape.39 = bf16[512,20,112]{2,1,0:T(8,128)(2,1)} reshape(bf16[2,4,64,2240]{3,2,1,0:T(8,128)(2,1)S(1)} %copy-done) | data formatting | bytes 4587520 | tf_op jit(solution)/shard_map/reshape | solution.py:66
  20.7 5.1 %fusion.9 = f32[20,112,112]{2,1,0:T(8,128)} fusion(bf16[512,20,112]{2,1,0:T(8,128)(2,1)} %reshape.39, bf16[512,20,112]{2,1,0:T(8,128)(2,1)} %max.13), kind=kOutput, calls=%fused_computation.17 | convolution fusion | flops 256901120 | bytes 5591040 | tf_op jit(solution)/shard_map/thd,the->hde/dot_general | solution.py:67
  25.8 0.0 all-gather.8.cloned.1.call-start
  25.9 0.7 copy.26
  26.6 22.9 %all-gather.1 = bf16[16,140,140]{2,1,0:T(8,128)(2,1)S(1)} all-gather(bf16[1,140,140]{2,1,0:T(8,128)(2,1)} %bitcast.29), channel_id=1, replica_groups=mesh['tm'=16,'space'=16] {'tm'}, dimensions={0}, use_global_device_ids=true | all-gather | bytes 666400 | tf_op jit(solution)/shard_map/all_gather | solution.py:90
  49.5 1.2 reshape.48
  50.7 2.3 copy.30
  53.1 87.8 %all-reduce.3.cloned.1.call-done = f32[20,112,112]{2,1,0:T(8,128)} async-done(((f32[20,112,112]{2,1,0:T(8,128)}), f32[20,112,112]{2,1,0:T(8,128)}) %all-reduce.3.cloned.1.call-update) | async-done | bytes 1003536 | tf_op jit(solution)/shard_map/psum | solution.py:70
  140.9 0.1 fusion.12
  141.0 2.2 collective-permute-start
  143.3 1.3 collective-permute-start.1
  144.6 0.2 slice_reduce_fusion.10
  144.8 1.6 broadcast_maximum_fusion
  146.4 0.7 collective-permute-done.1
  147.2 1.3 fusion.6
  148.5 5.9 %add_convert_fusion.1 = bf16[2,4,64,2240]{3,2,1,0:T(8,128)(2,1)} fusion(bf16[2,4,64,2240]{3,2,1,0:T(8,128)(2,1)S(1)} %copy-done, bf16[2,6,66,2240]{3,2,1,0:T(8,128)(2,1)S(1)} %fusion.6, bf16[2,1,64,2240]{3,2,1,0:T(8,128)(2,1)S(1)} %collective-permute-done.1, bf16[2,1,64,2240]{3,2,1,0:T(8,128)(2,1)S(1)} %collective-permute-done, ...), kind=kLoop, calls=%fused_computation.5 | loop fusion | flops 33259520 | bytes 19577600 | tf_op jit(solution)/shard_map/convert_element_type | solution.py:56
  154.3 1.3 collective-permute-start.2
  155.6 0.1 slice_reduce_fusion.11
  155.7 6.6 %max.15 = bf16[512,20,112]{2,1,0:T(8,128)(2,1)} reshape(bf16[2,4,64,2240]{3,2,1,0:T(8,128)(2,1)} %broadcast_maximum_fusion) | data formatting | bytes 4587520 | tf_op jit(solution)/shard_map/max | solution.py:74
  162.3 47.6 %all-gather.8.cloned.1.call-done = bf16[16,140,2240]{2,1,0:T(8,128)(2,1)} async-done(((bf16[1,140,2240]{2,1,0:T(8,128)(2,1)}), bf16[16,140,2240]{2,1,0:T(8,128)(2,1)}) %all-gather.8.cloned.1.call-update) | async-done | bytes 10035216 | tf_op jit(solution)/shard_map/all_gather | solution.py:93
  209.9 11.9 %reshape.47 = bf16[2240,2240]{1,0:T(8,128)(2,1)} reshape(bf16[16,140,2240]{2,1,0:T(8,128)(2,1)} %all-gather.8.cloned.1.call-done) | data formatting | bytes 20070400
  221.8 111.6 %all-gather.6.cloned.1.call-done = f32[320,112,112]{2,1,0:T(8,128)} async-done(((f32[20,112,112]{2,1,0:T(8,128)}), f32[320,112,112]{2,1,0:T(8,128)}) %all-gather.6.cloned.1.call-update) | async-done | bytes 16056336 | tf_op jit(solution)/shard_map/all_gather | solution.py:13
  333.3 0.1 broadcast_in_dim.2
  333.4 23.2 %while.10 = (s32[]{:T(128)}, f32[20,112,112]{2,1,0:T(8,128)S(1)}, s32[]{:T(128)}, f32[16,20,112,112]{3,2,1,0:T(8,128)}, s32[]{:T(128)}, /*index=5*/s32[]{:T(128)}, s32[]{:T(128)}) while((s32[]{:T(128)}, f32[20,112,112]{2,1,0:T(8,128)S(1)}, s32[]{:T(128)}, f32[16,20,112,112]{3,2,1,0:T(8,128)}, s32[]{:T(128)}, /*index=5*/s32[]{:T(128)}, ...), condition=%wide.region_2.3_spmd, body=%wide.region_1.2_spmd.sunk | while | flops 250885 | bytes 3010675 | solution.py:19
  333.4 1.6 bitcast_add_fusion.2
  335.0 1.5 bitcast_add_fusion.2
  336.6 1.5 bitcast_add_fusion.2
  338.1 1.5 bitcast_add_fusion.2
  339.6 1.5 bitcast_add_fusion.2
  341.2 1.5 bitcast_add_fusion.2
  342.7 1.5 bitcast_add_fusion.2
  344.2 1.5 bitcast_add_fusion.2
  345.7 1.5 bitcast_add_fusion.2
  347.3 1.5 bitcast_add_fusion.2
  348.8 1.5 bitcast_add_fusion.2
  350.3 1.5 bitcast_add_fusion.2
  351.8 1.5 bitcast_add_fusion.2
  353.4 1.5 bitcast_add_fusion.2
  354.9 1.5 bitcast_add_fusion.2
  356.6 2.9 fusion.4
  359.6 2.8 bitcast_multiply_fusion
  362.4 6.2 %copy.25 = f32[512,20,112]{2,1,0:T(8,128)} copy(f32[512,20,112]{0,2,1:T(8,128)} %bitcast_multiply_fusion) | data formatting | bytes 9175040 | tf_op jit(solution)/shard_map/mul | solution.py:77
  368.6 7.3 %reshape.40 = f32[2,4,64,2240]{3,2,1,0:T(8,128)} reshape(f32[512,20,112]{2,1,0:T(8,128)} %copy.25) | data formatting | bytes 9175040 | tf_op jit(solution)/shard_map/reshape | solution.py:77
  375.9 5.4 %add_convert_fusion = bf16[2,4,64,2240]{3,2,1,0:T(8,128)(2,1)S(1)} fusion(bf16[2,4,64,2240]{3,2,1,0:T(8,128)(2,1)} %collective-permute-done.2, bf16[2,4,64,2240]{3,2,1,0:T(8,128)(2,1)} %add_convert_fusion.1, f32[2,4,64,2240]{3,2,1,0:T(8,128)} %reshape.40, f32[2240]{0:T(1024)S(1)} %get-tuple-element.39, f32[2240]{0:T(1024)S(1)} %get-tuple-element.40, ...), kind=kLoop, calls=%fused_computation.4 | loop fusion | flops 13762560 | bytes 11504640 | tf_op jit(solution)/shard_map/convert_element_type | solution.py:89
  381.3 13.4 %convolution_convert_fusion = bf16[512,2240]{0,1:T(8,128)(2,1)} fusion(bf16[512,2240]{1,0:T(8,128)(2,1)S(1)} %bitcast.27, bf16[2240,2240]{1,0:T(8,128)(2,1)} %reshape.47), kind=kOutput, calls=%fused_computation.12 | convolution fusion | flops 5139169280 | bytes 14622720 | tf_op jit(solution)/shard_map/dot_general | solution.py:91
  394.7 4.2 %copy.28 = bf16[512,2240]{1,0:T(8,128)(2,1)} copy(bf16[512,2240]{0,1:T(8,128)(2,1)} %convolution_convert_fusion) | data formatting | bytes 4587520 | tf_op jit(solution)/shard_map/convert_element_type | solution.py:96
  (22 shorter events, 0.1 us)
Async XLA Ops:
  6.5 9.9 %copy-start = (bf16[2,4,64,2240]{3,2,1,0:T(8,128)(2,1)S(1)}, bf16[2,4,64,2240]{3,2,1,0:T(8,128)(2,1)}, u32[]{:S(2)}) copy-start(bf16[2,4,64,2240]{3,2,1,0:T(8,128)(2,1)} %param.11) | copy-start | bytes 6881284
  6.5 134.3 %all-reduce.3.cloned.1.call-start = ((), (), s32[]{:S(2)}) async-start(), calls=%async_computation | async-start | bytes 2293760 | tf_op jit(solution)/shard_map/psum | solution.py:70
  20.7 5.1 %copy-start.3 = (bf16[140,140]{1,0:T(8,128)(2,1)S(1)}, bf16[140,140]{1,0:T(8,128)(2,1)}, u32[]{:S(2)}) copy-start(bf16[140,140]{1,0:T(8,128)(2,1)} %param.15) | copy-start | bytes 117604
  25.8 184.0 %all-gather.8.cloned.1.call-start = ((), (), s32[]{:S(2)}) async-start(), calls=%async_computation.2 | async-start | bytes 11280384 | tf_op jit(solution)/shard_map/all_gather | solution.py:93
  50.7 93.8 %copy-start.4 = (f32[9,2240]{1,0:T(8,128)S(1)}, f32[9,2240]{1,0:T(8,128)}, u32[]{:S(2)}) copy-start(f32[9,2240]{1,0:T(8,128)} %param.13) | copy-start | bytes 241924
  53.0 280.3 %all-gather.6.cloned.1.call-start = ((), (), s32[]{:S(2)}) async-start(), calls=%async_computation.1 | async-start | bytes 19496960 | tf_op jit(solution)/shard_map/all_gather | solution.py:13
  140.9 3.9 copy-start.2
  141.0 5.4 %collective-permute-start = (bf16[2,1,64,2240]{3,2,1,0:T(8,128)(2,1)S(1)}, bf16[2,1,64,2240]{3,2,1,0:T(8,128)(2,1)S(1)}, u32[]{:S(2)}, u32[]{:S(2)}) collective-permute-start(bf16[2,1,64,2240]{3,2,1,0:T(8,128)(2,1)S(1)} %get-tuple-element.49), channel_id=1, source_target_pairs={{0,1},{1,2},{2,3},{3,4},{4,5},{5,6},{6,7},{7,8},{8,9},{9,10},{10,1... | collective-permute-start | bytes 1720328 | tf_op jit(solution)/shard_map/ppermute | solution.py:27
  143.3 3.9 collective-permute-start.1
  148.4 7.2 %copy-start.5 = (f32[3,2240]{1,0:T(4,128)S(1)}, f32[3,2240]{1,0:T(4,128)}, u32[]{:S(2)}) copy-start(f32[3,2240]{1,0:T(4,128)} %param.14) | copy-start | bytes 80644
  154.3 221.6 %collective-permute-start.2 = (bf16[2,4,64,2240]{3,2,1,0:T(8,128)(2,1)}, bf16[2,4,64,2240]{3,2,1,0:T(8,128)(2,1)}, u32[]{:S(2)}, u32[]{:S(2)}) collective-permute-start(bf16[2,4,64,2240]{3,2,1,0:T(8,128)(2,1)} %add_convert_fusion.1), channel_id=1, source_target_pairs={{0,16},{16,32},{32,48},{48,64},{64,80},{80,96},{96,112},{112,128},... | collective-permute-start | bytes 6881288 | tf_op jit(solution)/shard_map/ppermute | solution.py:38
  333.4 23.2 %copy-start.1 = (f32[20,112,112]{2,1,0:T(8,128)S(1)}, f32[20,112,112]{2,1,0:T(8,128)}, u32[]{:S(2)}) copy-start(f32[20,112,112]{2,1,0:T(8,128)} %all-reduce.3.cloned.1.call-done) | copy-start | bytes 3010564
  368.6 7.3 %copy-start.6 = (f32[2240]{0:T(1024)S(1)}, f32[2240]{0:T(1024)}, u32[]{:S(2)}) copy-start(f32[2240]{0:T(1024)} %param.12) | copy-start | bytes 26884
Sparse Core Ops, SparseCore 0:
  25.9 114.9 all-reduce.2
  142.7 67.0 all-gather.7
  212.3 120.9 all-gather.5
where the time goes:
time: 407 us; the launch traced here: 405 us
  waiting for transfers between devices  248 us (61%)
  local copies, waits for them, and re-layouts  51.7 us (13%)
  other arithmetic  42.9 us (11%)
  blocking collectives  22.9 us (6%)
  matrix products  21.4 us (5%)
  between operations  13.3 us (3%)
  starting transfers between devices  4.89 us (1%)
    all_gather x1, waiting for transfers between devices, entering(): gathered = lax.all_gather(part, axis)  112 us
    psum x1, waiting for transfers between devices, per_device(): summed = lax.psum(local_state, 'space')  87.8 us
    all_gather x1, waiting for transfers between devices, per_device(): lax.all_gather(weight_band, 'space', axis=0, tiled=True)  47.6 us
    all_gather x1, blocking collectives, per_device(): weight_band = lax.all_gather(out_weight, 'tm', axis=1, tiled=True)  22.9 us
    add x15, other arithmetic, add_states(): return earlier + latter  22.6 us
    unnamed x18, local copies, waits for them, and re-layouts  16.2 us
    dot_general x1, matrix products, per_device(): jnp.dot(mixed, lax.all_gather(weight_band, 'space', axis=0, tiled=True),...  13.4 us
  transfers between devices with their start and end apart: 6, of which 4 were waited for; matrix products, arithmetic and copies ran while one was open for 18% of the time, Pallas kernels for 0%

commit v1 on v0

--- a/solution.py
+++ b/solution.py
@@ -90,7 +90,12 @@
     weight_band = lax.all_gather(out_weight, "tm", axis=1, tiled=True)
     projected = jnp.dot(
         mixed,
-        lax.all_gather(weight_band, "space", axis=0, tiled=True),
+        jnp.concatenate(
+            lax.all_to_all(
+                jnp.stack([weight_band for _ in range(lax.axis_size("space"))]), "space", 0, 0
+            ),
+            axis=0,
+        ),
         preferred_element_type=jnp.float32,
     )
     return projected.astype(jnp.bfloat16).reshape(frame_count, row_count, col_count, model_width)

time: 407 us -> 512 us (1.26)
  the two profiles are of different devices: /device:TPU:30 before, /device:TPU:29 now
where the time goes in v1:
time: 512 us; the launch traced here: 511 us
  waiting for transfers between devices  344 us (67%)
  local copies, waits for them, and re-layouts  54 us (11%)
  other arithmetic  41.4 us (8%)
  starting transfers between devices  21.2 us (4%)
  blocking collectives  19.4 us (4%)
  matrix products  16.5 us (3%)
  between operations  13.6 us (3%)
    ppermute x1, waiting for transfers between devices, extended(): lax.ppermute(lax.slice_in_dim(block, block.shape[dim] - width, None, axis...  227 us
    psum x1, waiting for transfers between devices, per_device(): summed = lax.psum(local_state, 'space')  115 us
    add x14, other arithmetic, add_states(): return earlier + latter  21.1 us
    all_gather x1, blocking collectives, per_device(): weight_band = lax.all_gather(out_weight, 'tm', axis=1, tiled=True)  19.4 us
    all_to_all x1, starting transfers between devices, per_device(): lax.all_to_all(jnp.stack([weight_band for _ in range(lax.axis_size('space...  12.8 us
    reshape x1, local copies, waits for them, and re-layouts, per_device(): jnp.concatenate(lax.all_to_all(jnp.stack([weight_band for _ in range(lax....  11.9 us
  transfers between devices with their start and end apart: 6, of which 3 were waited for; matrix products, arithmetic and copies ran while one was open for 15% of the time, Pallas kernels for 0%

profile of v1, /device:TPU:29, one launch (start us, length us, event | category | flops | bytes accessed | tf_op | source)
XLA Modules:
  0.0 510.9 jit_solution(12124587281421820721)
XLA Ops:
  6.5 3.4 broadcast_maximum_fusion.1
  9.9 6.5 %max.13 = bf16[512,20,112]{2,1,0:T(8,128)(2,1)} reshape(bf16[2,4,64,2240]{3,2,1,0:T(8,128)(2,1)} %broadcast_maximum_fusion.1) | data formatting | bytes 4587520 | tf_op jit(solution)/shard_map/max | solution.py:68
  16.5 4.3 reshape.44
  20.7 5.0 fusion.9
  25.8 0.0 all-gather.4.cloned.1.call-start
  25.9 115.4 %all-reduce.3.cloned.1.call-done = f32[20,112,112]{2,1,0:T(8,128)} async-done(((f32[20,112,112]{2,1,0:T(8,128)}), f32[20,112,112]{2,1,0:T(8,128)}) %all-reduce.3.cloned.1.call-update) | async-done | bytes 1003536 | tf_op jit(solution)/shard_map/psum | solution.py:70
  141.3 0.7 copy.27
  142.0 19.4 %all-gather.1 = bf16[16,140,140]{2,1,0:T(8,128)(2,1)S(1)} all-gather(bf16[1,140,140]{2,1,0:T(8,128)(2,1)} %bitcast.27), channel_id=1, replica_groups=mesh['tm'=16,'space'=16] {'tm'}, dimensions={0}, use_global_device_ids=true | all-gather | bytes 666400 | tf_op jit(solution)/shard_map/all_gather | solution.py:90
  161.4 1.2 reshape.52
  162.6 1.6 copy.31
  164.3 4.6 stack.2
  168.9 12.8 %all-to-all-start = ((bf16[16,140,2240]{2,1,0:T(8,128)(2,1)}), bf16[16,140,2240]{2,1,0:T(8,128)(2,1)}, u32[]{:S(2)}, u32[]{:S(2)}) async-start(bf16[16,140,2240]{2,1,0:T(8,128)(2,1)} %stack.2), calls=%async_computation | async-start | bytes 21233664 | tf_op jit(solution)/shard_map/all_to_all | solution.py:94
  181.7 0.1 fusion.12
  181.8 3.7 collective-permute-start
  185.5 1.9 collective-permute-start.1
  187.4 0.2 slice_reduce_fusion.10
  187.7 1.6 broadcast_maximum_fusion
  189.3 227.2 %collective-permute-done = bf16[2,1,64,2240]{3,2,1,0:T(8,128)(2,1)S(1)} collective-permute-done((bf16[2,1,64,2240]{3,2,1,0:T(8,128)(2,1)S(1)}, bf16[2,1,64,2240]{3,2,1,0:T(8,128)(2,1)S(1)}, u32[]{:S(2)}, u32[]{:S(2)}) %collective-permute-start) | collective-permute-done | bytes 573472 | tf_op jit(solution)/shard_map/ppermute | solution.py:27
  416.5 1.7 collective-permute-done.1
  418.2 1.3 fusion.6
  419.5 5.9 %add_convert_fusion.1 = bf16[2,4,64,2240]{3,2,1,0:T(8,128)(2,1)} fusion(bf16[2,4,64,2240]{3,2,1,0:T(8,128)(2,1)S(1)} %copy-done, bf16[2,6,66,2240]{3,2,1,0:T(8,128)(2,1)S(1)} %fusion.6, bf16[2,1,64,2240]{3,2,1,0:T(8,128)(2,1)S(1)} %collective-permute-done.1, bf16[2,1,64,2240]{3,2,1,0:T(8,128)(2,1)S(1)} %collective-permute-done, ...), kind=kLoop, calls=%fused_computation.5 | loop fusion | flops 33259520 | bytes 19577600 | tf_op jit(solution)/shard_map/convert_element_type | solution.py:56
  425.4 2.8 collective-permute-start.2
  428.1 0.1 slice_reduce_fusion.11
  428.2 6.5 %max.15 = bf16[512,20,112]{2,1,0:T(8,128)(2,1)} reshape(bf16[2,4,64,2240]{3,2,1,0:T(8,128)(2,1)} %broadcast_maximum_fusion) | data formatting | bytes 4587520 | tf_op jit(solution)/shard_map/max | solution.py:74
  434.8 11.9 %reshape.47 = bf16[2240,2240]{1,0:T(8,128)(2,1)} reshape(bf16[16,140,2240]{2,1,0:T(8,128)(2,1)} %all-to-all-done) | data formatting | bytes 20070400 | tf_op jit(solution)/shard_map/reshape | solution.py:93
  446.7 0.1 broadcast_in_dim.2
  446.7 21.7 %while.10 = (s32[]{:T(128)}, f32[20,112,112]{2,1,0:T(8,128)S(1)}, s32[]{:T(128)}, f32[16,20,112,112]{3,2,1,0:T(8,128)}, s32[]{:T(128)}, /*index=5*/s32[]{:T(128)}, s32[]{:T(128)}) while((s32[]{:T(128)}, f32[20,112,112]{2,1,0:T(8,128)S(1)}, s32[]{:T(128)}, f32[16,20,112,112]{3,2,1,0:T(8,128)}, s32[]{:T(128)}, /*index=5*/s32[]{:T(128)}, ...), condition=%wide.region_2.3_spmd, body=%wide.region_1.2_spmd.sunk | while | flops 250885 | bytes 3010675 | solution.py:19
  446.8 1.6 bitcast_add_fusion.2
  448.4 1.5 bitcast_add_fusion.2
  449.9 1.5 bitcast_add_fusion.2
  451.4 1.5 bitcast_add_fusion.2
  453.0 1.5 bitcast_add_fusion.2
  454.5 1.5 bitcast_add_fusion.2
  456.0 1.5 bitcast_add_fusion.2
  457.5 1.5 bitcast_add_fusion.2
  459.1 1.5 bitcast_add_fusion.2
  460.6 1.5 bitcast_add_fusion.2
  462.1 1.5 bitcast_add_fusion.2
  463.7 1.5 bitcast_add_fusion.2
  465.2 1.5 bitcast_add_fusion.2
  466.7 1.5 bitcast_add_fusion.2
  468.4 3.0 fusion.4
  471.4 2.8 bitcast_multiply_fusion
  474.2 6.2 %copy.26 = f32[512,20,112]{2,1,0:T(8,128)} copy(f32[512,20,112]{0,2,1:T(8,128)} %bitcast_multiply_fusion) | data formatting | bytes 9175040 | tf_op jit(solution)/shard_map/mul | solution.py:77
  480.4 7.3 %reshape.45 = f32[2,4,64,2240]{3,2,1,0:T(8,128)} reshape(f32[512,20,112]{2,1,0:T(8,128)} %copy.26) | data formatting | bytes 9175040 | tf_op jit(solution)/shard_map/reshape | solution.py:77
  487.7 5.4 %add_convert_fusion = bf16[2,4,64,2240]{3,2,1,0:T(8,128)(2,1)S(1)} fusion(bf16[2,4,64,2240]{3,2,1,0:T(8,128)(2,1)} %collective-permute-done.2, bf16[2,4,64,2240]{3,2,1,0:T(8,128)(2,1)} %add_convert_fusion.1, f32[2,4,64,2240]{3,2,1,0:T(8,128)} %reshape.45, f32[2240]{0:T(1024)S(1)} %get-tuple-element.39, f32[2240]{0:T(1024)S(1)} %get-tuple-element.40, ...), kind=kLoop, calls=%fused_computation.4 | loop fusion | flops 13762560 | bytes 11504640 | tf_op jit(solution)/shard_map/convert_element_type | solution.py:89
  493.1 8.5 %convolution_convert_fusion = bf16[512,2240]{0,1:T(8,128)(2,1)S(1)} fusion(bf16[512,2240]{1,0:T(8,128)(2,1)S(1)} %bitcast.25, bf16[2240,2240]{1,0:T(8,128)(2,1)} %reshape.47), kind=kOutput, calls=%fused_computation.12 | convolution fusion | flops 5139169280 | bytes 14622720 | tf_op jit(solution)/shard_map/dot_general | solution.py:91
  501.5 2.5 copy.29
  (21 shorter events, 0.1 us)
Async XLA Ops:
  6.5 9.9 %copy-start = (bf16[2,4,64,2240]{3,2,1,0:T(8,128)(2,1)S(1)}, bf16[2,4,64,2240]{3,2,1,0:T(8,128)(2,1)}, u32[]{:S(2)}) copy-start(bf16[2,4,64,2240]{3,2,1,0:T(8,128)(2,1)} %param.11) | copy-start | bytes 6881284
  6.5 134.7 %all-reduce.3.cloned.1.call-start = ((), (), s32[]{:S(2)}) async-start(), calls=%async_computation.1 | async-start | bytes 2293760 | tf_op jit(solution)/shard_map/psum | solution.py:70
  20.7 120.5 %copy-start.3 = (bf16[140,140]{1,0:T(8,128)(2,1)S(1)}, bf16[140,140]{1,0:T(8,128)(2,1)}, u32[]{:S(2)}) copy-start(bf16[140,140]{1,0:T(8,128)(2,1)} %param.15) | copy-start | bytes 117604
  25.8 420.8 %all-gather.4.cloned.1.call-start = ((), (), s32[]{:S(2)}) async-start(), calls=%async_computation.2 | async-start | bytes 19496960 | tf_op jit(solution)/shard_map/all_gather | solution.py:13
  168.9 18.5 %copy-start.4 = (f32[9,2240]{1,0:T(8,128)S(1)}, f32[9,2240]{1,0:T(8,128)}, u32[]{:S(2)}) copy-start(f32[9,2240]{1,0:T(8,128)} %param.13) | copy-start | bytes 241924
  168.9 265.8 %all-to-all-start = ((bf16[16,140,2240]{2,1,0:T(8,128)(2,1)}), bf16[16,140,2240]{2,1,0:T(8,128)(2,1)}, u32[]{:S(2)}, u32[]{:S(2)}) async-start(bf16[16,140,2240]{2,1,0:T(8,128)(2,1)} %stack.2), calls=%async_computation | async-start | bytes 21233664 | tf_op jit(solution)/shard_map/all_to_all | solution.py:94
  181.7 5.9 %copy-start.2 = (bf16[2,4,64,2240]{3,2,1,0:T(8,128)(2,1)S(1)}, bf16[2,4,64,2240]{3,2,1,0:T(8,128)(2,1)}, u32[]{:S(2)}) copy-start(bf16[2,4,64,2240]{3,2,1,0:T(8,128)(2,1)} %param.9) | copy-start | bytes 6881284
  181.8 234.7 %collective-permute-start = (bf16[2,1,64,2240]{3,2,1,0:T(8,128)(2,1)S(1)}, bf16[2,1,64,2240]{3,2,1,0:T(8,128)(2,1)S(1)}, u32[]{:S(2)}, u32[]{:S(2)}) collective-permute-start(bf16[2,1,64,2240]{3,2,1,0:T(8,128)(2,1)S(1)} %get-tuple-element.49), channel_id=1, source_target_pairs={{0,1},{1,2},{2,3},{3,4},{4,5},{5,6},{6,7},{7,8},{8,9},{9,10},{10,1... | collective-permute-start | bytes 1720328 | tf_op jit(solution)/shard_map/ppermute | solution.py:27
  185.5 232.7 %collective-permute-start.1 = (bf16[2,1,64,2240]{3,2,1,0:T(8,128)(2,1)S(1)}, bf16[2,1,64,2240]{3,2,1,0:T(8,128)(2,1)S(1)}, u32[]{:S(2)}, u32[]{:S(2)}) collective-permute-start(bf16[2,1,64,2240]{3,2,1,0:T(8,128)(2,1)S(1)} %get-tuple-element.50), channel_id=1, source_target_pairs={{1,0},{2,1},{3,2},{4,3},{5,4},{6,5},{7,6},{8,7},{9,8},{10,9},{11,1... | collective-permute-start | bytes 1720328 | tf_op jit(solution)/shard_map/ppermute | solution.py:30
  419.5 8.6 %copy-start.5 = (f32[3,2240]{1,0:T(4,128)S(1)}, f32[3,2240]{1,0:T(4,128)}, u32[]{:S(2)}) copy-start(f32[3,2240]{1,0:T(4,128)} %param.14) | copy-start | bytes 80644
  425.4 62.3 %collective-permute-start.2 = (bf16[2,4,64,2240]{3,2,1,0:T(8,128)(2,1)}, bf16[2,4,64,2240]{3,2,1,0:T(8,128)(2,1)}, u32[]{:S(2)}, u32[]{:S(2)}) collective-permute-start(bf16[2,4,64,2240]{3,2,1,0:T(8,128)(2,1)} %add_convert_fusion.1), channel_id=1, source_target_pairs={{0,16},{16,32},{32,48},{48,64},{64,80},{80,96},{96,112},{112,128},... | collective-permute-start | bytes 6881288 | tf_op jit(solution)/shard_map/ppermute | solution.py:38
  446.7 21.7 %copy-start.1 = (f32[20,112,112]{2,1,0:T(8,128)S(1)}, f32[20,112,112]{2,1,0:T(8,128)}, u32[]{:S(2)}) copy-start(f32[20,112,112]{2,1,0:T(8,128)} %all-reduce.3.cloned.1.call-done) | copy-start | bytes 3010564
  480.4 7.3 %copy-start.6 = (f32[2240]{0:T(1024)S(1)}, f32[2240]{0:T(1024)}, u32[]{:S(2)}) copy-start(f32[2240]{0:T(1024)} %param.12) | copy-start | bytes 26884
Sparse Core Ops, SparseCore 0:
  25.9 115.2 all-reduce.2
  143.7 148.7 all-gather.3
